TPU v7x, 256 devices: a whole 4x4x8 slice. The times are simulated.
256 devices in a mesh: dp: 16 (over z_lo, x), tensor: 16 (over y, z_hi, core).
Axes of the slice: x: 4, y: 4, z: 8 (z_hi: 2, z_lo: 4; z = z_hi * 4 + z_lo), core: 2. Of those that a mesh axis runs over, the one named last changes fastest.
Arguments:
- inner_x: bfloat16 [16, 2048, 7168], P('dp', None, 'tensor')
- gate_z: bfloat16 [16, 2048, 7168], P('dp', None, 'tensor'), may hold values from -6 to 6
- input_b: bfloat16 [16, 2048, 128], P('dp'), may hold values from -0.75 to 0.75
- output_c: bfloat16 [16, 2048, 128], P('dp'), may hold values from -6 to 6
- step_raw: float32 [16, 2048, 112], P('dp', None, 'tensor'), may hold values from -6 to 6
- decay_rate: float32 [112], P('tensor'), may hold values from 0.001 to 0.05
- skip_gain: float32 [112], P('tensor'), may hold values from 0.5 to 1.5
- norm_gain: float32 [7168], P('tensor'), may hold values from 0.5 to 1.5
- out_weight: bfloat16 [7168, 3584], P('tensor'), may hold values from -0.0625 to 0.0625
- segment: int32 [16, 2048], P('dp'), may hold values from 0 to 7, never falling along the last dimension, each value on 1 to 1024 neighbouring positions
- cache_slot: int32 [16, 8], replicated, may hold values from 0 to 127, as said below
Outputs:
- mixed: bfloat16 [16, 2048, 3584], P('dp', 'tensor')
- cache: float32 [128, 112, 4096], P('dp', 'tensor')
Inputs may be any that keep to these rules, and one draw needn't show every extreme that they name: `segment`: in each group's row the prompt numbers never fall and every prompt 0 to 7 is present. `cache_slot`: every slot is named exactly once; slot // 8 is the owning group, and no two prompts of one group have the same owning group.
All inputs are finite; a program needn't handle non-finite values.
Results may differ from a plain program's by a relative error of at most 0.018.
Values may be sent and summed in bfloat16 or wider, within the bound.
No kernel may reach another device: no remote copies, remote signals or barrier semaphores. Data moves between devices by JAX's collectives and lax.ppermute only.
A program may use at most 192 MiB of HBM per device.

v0:
```python
import jax
import jax.numpy as jnp
from jax import lax
from jax.sharding import Mesh, PartitionSpec as P

HEADS = 112
HEAD = 64
STATE = 64
NGROUPS = 2
REQS = 8
BLOCK = 256
INNER = 7168
HIGHEST = lax.Precision.HIGHEST
TENSOR = ("head_group", "y_rest", "z_hi", "core")
GROUP_MATES = TENSOR[1:]
NEAR_FIRST = ("head_group", "y_rest", "core")
FAR_LAST = "z_hi"


def split_pair(values):
    upper = values.astype(jnp.bfloat16)
    lower = (values - upper.astype(jnp.float32)).astype(jnp.bfloat16)
    return (upper, lower)


def split_einsum(form, wide, narrow):
    upper, lower = split_pair(wide)
    first = jnp.einsum(form, upper, narrow, preferred_element_type=jnp.float32)
    return first + jnp.einsum(form, lower, narrow, preferred_element_type=jnp.float32)


def local(
    inner_x,
    gate_z,
    input_b,
    output_c,
    step_raw,
    decay_rate,
    skip_gain,
    norm_gain,
    out_weight,
    segment,
    cache_slot,
):
    stream_len = inner_x.shape[1]
    dev_width = inner_x.shape[2]
    dev_heads = decay_rate.shape[0]
    tensor_idx = lax.axis_index(TENSOR)
    group_idx = tensor_idx * dev_heads // (HEADS // NGROUPS)
    b_cols = lax.dynamic_slice_in_dim(input_b[0], group_idx * STATE, STATE, 1)
    c_cols = lax.dynamic_slice_in_dim(output_c[0], group_idx * STATE, STATE, 1)
    step_size = jax.nn.softplus(step_raw[0])
    cum_log = jnp.cumsum(-decay_rate[None, :] * step_size, axis=0)
    seg_row = segment[0]
    block_count = stream_len // BLOCK
    x_blk = inner_x[0].reshape(block_count, BLOCK, dev_heads, HEAD)
    cum_blk = cum_log.reshape(block_count, BLOCK, dev_heads)
    step_blk = step_size.reshape(block_count, BLOCK, dev_heads)
    seg_blk = seg_row.reshape(block_count, BLOCK)
    b_blk = b_cols.reshape(block_count, BLOCK, STATE)
    c_blk = c_cols.reshape(block_count, BLOCK, STATE)
    positions = jnp.arange(BLOCK)
    scores = jnp.einsum("btn,bsn->bts", c_blk, b_blk, preferred_element_type=jnp.float32)
    causal_mask = (positions[None, None, :] <= positions[None, :, None]) & (
        seg_blk[:, :, None] == seg_blk[:, None, :]
    )
    cum_t = cum_blk.transpose(0, 2, 1)
    log_gap = cum_t[:, :, :, None] - cum_t[:, :, None, :]
    weights = (
        jnp.exp(jnp.where(causal_mask[:, None], log_gap, -jnp.inf))
        * step_blk.transpose(0, 2, 1)[:, :, None, :]
        * scores[:, None]
    )
    intra_part = split_einsum("bhts,bshp->bthp", weights, x_blk)
    last_seg = seg_blk[:, -1]
    last_cum = cum_blk[:, -1]
    pull_back = (
        jnp.exp(last_cum[:, None, :] - cum_blk)
        * step_blk
        * (seg_blk == last_seg[:, None]).astype(jnp.float32)[:, :, None]
    )
    added = split_einsum("bshp,bsn->bhpn", pull_back[:, :, :, None] * x_blk, b_blk)
    prev_cum = jnp.concatenate([jnp.zeros((1, dev_heads), jnp.float32), last_cum[:-1]], axis=0)
    prev_seg = jnp.concatenate([jnp.full((1,), -1, seg_row.dtype), last_seg[:-1]], axis=0)
    blocks = jnp.arange(block_count)
    earlier = blocks[None, :] < blocks[:, None]
    mix_ok = earlier & (last_seg[None, :] == prev_seg[:, None])
    mix_gap = prev_cum[:, None, :] - last_cum[None, :, :]
    mix = jnp.exp(jnp.where(mix_ok[:, :, None], mix_gap, -jnp.inf))
    carried = jnp.sum(mix[:, :, :, None, None] * added[None], axis=1)
    live_rows = (seg_blk == prev_seg[:, None]).astype(jnp.float32)
    carry_decay = jnp.exp(cum_blk - prev_cum[:, None, :]) * live_rows[:, :, None]
    carry_part = split_einsum("bhpn,btn->bthp", carried, c_blk) * carry_decay[:, :, :, None]
    outputs = intra_part + carry_part + skip_gain[None, None, :, None] * x_blk.astype(jnp.float32)
    mixer_y = outputs.reshape(stream_len, dev_width)
    members = (seg_row[None, :] == jnp.arange(REQS)[:, None]).astype(jnp.float32)
    end_index = (
        jnp.sum((seg_row[None, :] <= jnp.arange(REQS)[:, None]).astype(jnp.int32), axis=1) - 1
    )
    at_end = (jnp.arange(stream_len)[None, :] == end_index[:, None]).astype(jnp.float32)
    end_cum = jnp.dot(at_end, cum_log, precision=HIGHEST)
    seg_end_cum = jnp.dot(members.T, end_cum, precision=HIGHEST)
    pull_all = jnp.exp(seg_end_cum - cum_log) * step_size
    weighted = (inner_x[0].reshape(stream_len, dev_heads, HEAD) * pull_all[:, :, None]).reshape(
        stream_len, dev_width
    )
    masked_b = (
        (members.astype(jnp.bfloat16)[:, :, None] * b_cols[None])
        .transpose(1, 0, 2)
        .reshape(stream_len, REQS * STATE)
    )
    finals = split_einsum("tc,tk->ck", weighted, masked_b)
    finals = (
        finals.reshape(dev_heads, HEAD, REQS, STATE)
        .transpose(2, 0, 1, 3)
        .reshape(REQS, dev_heads * HEAD * STATE)
    )
    gated = mixer_y * jax.nn.silu(gate_z[0].astype(jnp.float32))
    sum_sq = jnp.sum(gated * gated, axis=1)
    group_stat = lax.all_gather(sum_sq, GROUP_MATES, tiled=True)
    mean_sq = jnp.sum(group_stat.reshape(-1, stream_len), axis=0) / (INNER // NGROUPS)
    rounded = (gated * lax.rsqrt(mean_sq + 1e-05)[:, None] * norm_gain[None, :]).astype(
        jnp.bfloat16
    )
    sizes = [lax.axis_size(name) for name in TENSOR]
    rows = stream_len // (sizes[0] * sizes[1] * sizes[2] * sizes[3])
    reordered = (
        rounded.reshape(sizes[0], sizes[1], sizes[2], sizes[3], rows, dev_width)
        .transpose(0, 1, 3, 2, 4, 5)
        .reshape(stream_len, dev_width)
    )
    partial = jnp.dot(reordered, out_weight, preferred_element_type=jnp.float32).astype(
        jnp.bfloat16
    )
    near = lax.psum_scatter(partial, NEAR_FIRST, scatter_dimension=0, tiled=True)
    mixed = near
    dp_idx = lax.axis_index("dp")
    dp_size = lax.axis_size("dp")
    own_slots = lax.dynamic_slice_in_dim(cache_slot, dp_idx, 1, 0)[0]
    dest_hot = ((own_slots // REQS)[:, None] == jnp.arange(dp_size)[None, :]).astype(jnp.float32)
    outbound = jnp.dot(dest_hot.T, finals, precision=HIGHEST).reshape(
        dp_size, dev_heads, HEAD * STATE
    )
    inbound = lax.all_to_all(
        outbound.astype(jnp.bfloat16), "dp", split_axis=0, concat_axis=0, tiled=True
    ).astype(outbound.dtype)
    near, inbound = lax.optimization_barrier((mixed, inbound))
    far_idx = lax.axis_index(FAR_LAST)
    half = near.shape[0] // 2
    keep = lax.dynamic_slice_in_dim(near, far_idx * half, half, 0)
    send = lax.dynamic_slice_in_dim(near, (1 - far_idx) * half, half, 0)
    got = lax.ppermute(send, FAR_LAST, perm=[(0, 1), (1, 0)])
    projected = (keep.astype(jnp.float32) + got.astype(jnp.float32)).astype(jnp.bfloat16)
    mixed = projected[None]
    wanted = dp_idx * REQS + jnp.arange(REQS)
    take_hot = jnp.any(cache_slot[:, :, None] == wanted[None, None, :], axis=1).astype(jnp.float32)
    cache = jnp.dot(
        take_hot.T, inbound.reshape(dp_size, dev_heads * HEAD * STATE), precision=HIGHEST
    )
    return (mixed, cache.reshape(REQS, dev_heads, HEAD * STATE))


def solution(mesh):
    dp_size, tensor_size = mesh.devices.shape
    groups = NGROUPS
    rest = tensor_size // (2 * 2 * groups)
    split = Mesh(mesh.devices.reshape(dp_size, groups, rest, 2, 2), ("dp",) + TENSOR)
    tp = TENSOR
    in_specs = (
        P("dp", None, tp),
        P("dp", None, tp),
        P("dp", None, None),
        P("dp", None, None),
        P("dp", None, tp),
        P(tp),
        P(tp),
        P(tp),
        P(tp, None),
        P("dp", None),
        P(),
    )
    out_specs = (P("dp", tp, None), P("dp", tp, None))
    return jax.shard_map(local, mesh=split, in_specs=in_specs, out_specs=out_specs, check_vma=False)
```

profile of v0, /device:TPU:32, one launch (start us, length us, event | category | flops | bytes accessed | tf_op | source)
XLA Modules:
  0.0 264.6 jit_solution(3308803690519148081)
XLA Ops:
  7.2 0.5 broadcast.237
  7.8 1.4 reduce.9
  9.3 0.7 neg.23
  10.0 0.9 multiply_bitcast_fusion
  10.9 2.0 reduce-window.6
  12.9 0.2 slice_reduce_fusion
  13.1 0.2 reduce-window.9
  13.3 0.6 copy-done.8
  14.3 0.9 dynamic-slice_reduce_fusion
  15.2 0.5 and_select_fusion
  15.7 0.7 compare_convert_fusion
  16.4 0.7 fusion.51
  17.0 0.6 copy.328
  17.7 0.6 iota_compare_fusion
  18.3 3.3 %copy.253 = bf16[56,8,8,256]{3,2,1,0:T(8,128)(2,1)} copy(bf16[56,8,8,256]{3,1,2,0:T(8,128)(2,1)} %bitcast.156) | data formatting | bytes 3670016
  21.7 0.1 copy.246
  21.8 0.8 reduce.3
  22.6 0.1 copy.247
  22.7 2.6 constant_dynamic-slice_fusion.1
  25.3 1.2 copy.243
  26.6 1.0 copy.193
  27.6 1.3 compare_and_fusion
  29.0 1.5 fusion.39
  30.5 0.7 exponential_multiply_fusion
  31.2 6.7 %fusion.4 = f32[8,7,256,64]{2,3,1,0:T(8,128)} fusion(f32[8,256,256]{2,1,0:T(8,128)S(1)} %fusion.39, f32[8,7,256]{2,1,0:T(8,128)S(1)} %get-tuple-element.10, f32[8,7,256]{2,1,0:T(8,128)S(1)} %copy.193, pred[8,256,256]{2,1,0:T(8,128)(4,1)S(1)} %compare_and_fusion, bf16[8,256,7,64]{1,0,3,2:T(8,128)(2,1)S(1)} %bitcast.150), kind=kOutput, calls=%fused_computation.7 | convolution fusion | flops 488112128 | bytes 8241152 | tf_op jit(solution)/shard_map/bhts,bshp->bthp/dot_general | solution.py:28
  37.9 6.9 %fusion.1 = f32[8,7,256,64]{2,3,1,0:T(8,128)} fusion(f32[8,256,256]{2,1,0:T(8,128)S(1)} %fusion.39, f32[8,7,256]{2,1,0:T(8,128)S(1)} %get-tuple-element.10, f32[8,7,256]{2,1,0:T(8,128)S(1)} %copy.193, pred[8,256,256]{2,1,0:T(8,128)(4,1)S(1)} %compare_and_fusion, bf16[8,256,7,64]{1,0,3,2:T(8,128)(2,1)S(1)} %bitcast.151), kind=kOutput, calls=%fused_computation.5 | convolution fusion | flops 499122176 | bytes 8241152 | tf_op jit(solution)/shard_map/bhts,bshp->bthp/dot_general | solution.py:29
  44.7 2.3 convert_element_type.197
  47.0 5.7 %reshape.356 = f32[2,2,2,2,128,448]{4,3,2,1,0,5:T(2,128)} reshape(bf16[1,2048,448]{1,2,0:T(8,128)(2,1)} %param.12) | data formatting | bytes 5505024 | tf_op jit(solution)/shard_map/convert_element_type | solution.py:118
  52.8 3.9 %copy.254 = f32[56,8,8,256]{3,2,1,0:T(8,128)S(1)} copy(f32[56,8,8,256]{3,1,2,0:T(8,128)} %bitcast.148) | data formatting | bytes 7340032
  56.7 0.7 fusion.18
  57.4 0.6 fusion.28
  58.1 1.8 multiply_reduce_fusion
  59.9 0.6 fusion.37
  60.6 0.2 copy-done.14
  60.8 1.2 copy-done.22
  62.0 4.5 %multiply_reduce_fusion.1 = (f32[8,256]{1,0:T(8,128)S(1)}, f32[8,256,7,64]{1,3,2,0:T(8,128)}) fusion(f32[8,256,7,64]{1,0,3,2:T(8,128)S(1)} %bitcast.161, bf16[8,256,7,64]{1,0,3,2:T(8,128)(2,1)S(1)} %bitcast.154, f32[7]{0:T(128)S(1)} %copy-done.21, f32[8,256,7]{1,2,0:T(8,128)S(1)} %copy-done.14, f32[8,256,7,64]{1,3,2,0:T(8,128)S(1)} %fusion.37, ...), kind=kOutput, calls=%fused_computation.24 | convolution fusion | flops 131201024 | bytes 21430300 | tf_op jit(solution)/shard_map/bhpn,btn->bthp/dot_general | solution.py:29
  66.5 21.6 %all_gather.3 = f32[16384]{0:T(1024)} all-gather(f32[2048]{0:T(1024)S(1)} %bitcast.185), channel_id=1, replica_groups=mesh['dp'=16,'head_group'=2,'y_rest'=2,'z_hi'=2,'core'=2] {'y_rest','z_h..., dimensions={0}, use_global_device_ids=true | all-gather | bytes 73728 | tf_op jit(solution)/shard_map/all_gather | solution.py:120
  88.1 0.9 reshape.351
  89.0 5.4 %reshape.350 = f32[2,2,2,2,128,448]{4,3,5,2,1,0:T(2,128)} reshape(f32[8,256,7,64]{1,3,2,0:T(8,128)} %get-tuple-element.14) | data formatting | bytes 7340032 | tf_op jit(solution)/shard_map/reshape | solution.py:95
  94.5 4.9 %fusion.27 = bf16[2,2,2,2,128,448]{4,5,2,3,1,0:T(8,128)(2,1)S(1)} fusion(f32[448]{0:T(512)S(1)} %copy-done.19, f32[2,2,2,2,128]{4,3,2,1,0:T(2,128)S(1)} %bitcast.186, f32[2,2,2,2,128,448]{4,3,2,1,0,5:T(2,128)} %reshape.356, f32[2,2,2,2,128,448]{4,3,5,2,1,0:T(2,128)} %reshape.350), kind=kLoop, calls=%fused_computation.38 | loop fusion | flops 7340032 | bytes 9185024 | tf_op jit(solution)/shard_map/transpose | solution.py:129
  99.3 3.1 %copy.222 = bf16[2,2,2,2,128,448]{4,3,2,1,0,5:T(2,128)(2,1)} copy(bf16[2,2,2,2,128,448]{4,5,2,3,1,0:T(8,128)(2,1)S(1)} %fusion.27) | data formatting | bytes 3670016 | tf_op jit(solution)/shard_map/transpose | solution.py:129
  102.5 5.3 %reshape.352 = bf16[2048,448]{0,1:T(8,128)(2,1)} reshape(bf16[2,2,2,2,128,448]{4,3,2,1,0,5:T(2,128)(2,1)} %copy.222) | data formatting | bytes 3670016 | tf_op jit(solution)/shard_map/reshape | solution.py:130
  107.7 12.6 %convolution_convert_fusion = bf16[2048,3584]{1,0:T(8,128)(2,1)} fusion(bf16[2048,448]{0,1:T(8,128)(2,1)} %reshape.352, bf16[448,3584]{1,0:T(8,128)(2,1)S(1)} %copy-done), kind=kOutput, calls=%fused_computation | convolution fusion | flops 6584008704 | bytes 19726336 | tf_op jit(solution)/shard_map/dot_general | solution.py:132
  120.4 0.7 copy-done.13
  121.2 0.2 fusion.47
  121.3 1.1 fusion.17
  122.5 0.2 broadcast_multiply_fusion
  122.7 0.7 fusion.12
  123.4 1.1 fusion.58
  124.6 2.1 convolution_add_fusion
  126.6 2.6 reshape.353
  129.3 3.1 %copy.324 = f32[7,64,8,64]{3,1,0,2:T(8,128)} copy(f32[7,64,8,64]{3,2,1,0:T(8,128)} %reshape.353) | data formatting | bytes 1835008 | tf_op jit(solution)/shard_map/reshape | solution.py:114
  132.3 3.0 %reshape.354 = f32[8,28672]{1,0:T(8,128)} reshape(f32[8,7,64,64]{3,2,1,0:T(8,128)} %bitcast.155) | data formatting | bytes 1835008 | tf_op jit(solution)/shard_map/reshape | solution.py:116
  135.3 2.3 convolution_convert_fusion.1
  137.6 1.5 copy.224
  139.1 8.4 %all-to-all-start = ((bf16[16,7,4096]{2,1,0:T(8,128)(2,1)}), bf16[16,7,4096]{2,1,0:T(8,128)(2,1)}, u32[]{:S(2)}, u32[]{:S(2)}) async-start(bf16[16,7,4096]{2,1,0:T(8,128)(2,1)} %copy.224), calls=%async_computation.1 | async-start | bytes 2097152 | tf_op jit(solution)/shard_map/all_to_all | solution.py:144
  147.5 26.5 %all-to-all-done = bf16[16,7,4096]{2,1,0:T(8,128)(2,1)} async-done(((bf16[16,7,4096]{2,1,0:T(8,128)(2,1)}), bf16[16,7,4096]{2,1,0:T(8,128)(2,1)}, u32[]{:S(2)}, u32[]{:S(2)}) %all-to-all-start) | async-done | bytes 917536 | tf_op jit(solution)/shard_map/all_to_all | solution.py:144
  174.0 2.8 %convert_element_type.193 = f32[16,7,4096]{2,1,0:T(8,128)} convert(bf16[16,7,4096]{2,1,0:T(8,128)(2,1)} %all-to-all-done) | non-fusion elementwise | flops 458752 | bytes 2752512 | tf_op jit(solution)/shard_map/convert_element_type | solution.py:146
  176.8 30.8 %reduce-scatter.2.cloned.1.call-done = bf16[256,3584]{1,0:T(8,128)(2,1)} async-done(((bf16[2048,3584]{1,0:T(8,128)(2,1)}), bf16[256,3584]{1,0:T(8,128)(2,1)}) %reduce-scatter.2.cloned.1.call-update) | async-done | bytes 1835024 | tf_op jit(solution)/shard_map/reduce_scatter | solution.py:135
  207.6 2.2 constant_dynamic-slice_fusion
  209.7 4.8 %collective-permute-start = (bf16[128,3584]{1,0:T(8,128)(2,1)}, bf16[128,3584]{1,0:T(8,128)(2,1)}, u32[]{:S(2)}, u32[]{:S(2)}) collective-permute-start(bf16[128,3584]{1,0:T(8,128)(2,1)} %constant_dynamic-slice_fusion), channel_id=1, source_target_pairs={{0,2},{2,0},{1,3},{3,1},{4,6},{6,4},{5,7},{7,5},{8,10},{10,8},{9,1... | collective-permute-start | bytes 2752520 | tf_op jit(solution)/shard_map/ppermute | solution.py:152
  214.7 4.2 %fusion.20 = f32[8,7,4096]{2,0,1:T(8,128)} fusion(pred[16,8]{0,1:T(8,128)(4,1)S(1)} %compare_reduce_fusion, f32[2,8,7,4096]{3,2,1,0:T(8,128)} %bitcast.149), kind=kOutput, calls=%fused_computation.30 | convolution fusion | flops 44040192 | bytes 2752640 | tf_op jit(solution)/shard_map/dot_general | solution.py:157
  218.8 36.3 %collective-permute-done = bf16[128,3584]{1,0:T(8,128)(2,1)} collective-permute-done((bf16[128,3584]{1,0:T(8,128)(2,1)}, bf16[128,3584]{1,0:T(8,128)(2,1)}, u32[]{:S(2)}, u32[]{:S(2)}) %collective-permute-start) | collective-permute-done | bytes 917536 | tf_op jit(solution)/shard_map/ppermute | solution.py:152
  255.2 2.6 fusion.35
  (68 shorter events, 1.2 us)
Async XLA Ops:
  7.2 100.6 %copy-start = (bf16[448,3584]{1,0:T(8,128)(2,1)S(1)}, bf16[448,3584]{1,0:T(8,128)(2,1)}, u32[]{:S(2)}) copy-start(bf16[448,3584]{1,0:T(8,128)(2,1)} %param.19) | copy-start | bytes 9633796
  7.2 14.6 %copy-start.12 = (f32[1,2048,7]{1,0,2:T(1,128)S(1)}, f32[1,2048,7]{1,0,2:T(1,128)}, u32[]{:S(2)}) copy-start(f32[1,2048,7]{1,0,2:T(1,128)} %param.15) | copy-start | bytes 172036
  7.2 200.4 %reduce-scatter.2.cloned.1.call-start = ((), (), s32[]{:S(2)}) async-start(), calls=%async_computation.2 | async-start | bytes 16515072 | tf_op jit(solution)/shard_map/reduce_scatter | solution.py:135
  13.3 0.6 copy-start.8
  26.5 3.9 %copy-start.11 = (f32[2048,7]{0,1:T(8,128)S(1)}, f32[2048,7]{0,1:T(8,128)}, u32[]{:S(2)}) copy-start(f32[2048,7]{0,1:T(8,128)} %reduce.3) | copy-start | bytes 172036
  26.5 3.9 %copy-start.15 = (f32[8,256]{1,0:T(8,128)S(1)}, f32[8,256]{1,0:T(8,128)}, u32[]{:S(2)}) copy-start(f32[8,256]{1,0:T(8,128)} %get-tuple-element.11) | copy-start | bytes 24580
  26.5 3.9 %copy-start.16 = (f32[8,256]{1,0:T(8,128)S(1)}, f32[8,256]{1,0:T(8,128)}, u32[]{:S(2)}) copy-start(f32[8,256]{1,0:T(8,128)} %get-tuple-element.12) | copy-start | bytes 24580
  26.5 4.7 %copy-start.1 = (bf16[56,8,8,256]{3,2,1,0:T(8,128)(2,1)S(1)}, bf16[56,8,8,256]{3,2,1,0:T(8,128)(2,1)}, u32[]{:S(2)}) copy-start(bf16[56,8,8,256]{3,2,1,0:T(8,128)(2,1)} %copy.253) | copy-start | bytes 5505028
  26.6 2.3 copy-start.6
  37.9 6.9 %copy-start.4 = (bf16[1,2048,448]{1,2,0:T(8,128)(2,1)S(1)}, bf16[1,2048,448]{1,2,0:T(8,128)(2,1)}, u32[]{:S(2)}) copy-start(bf16[1,2048,448]{1,2,0:T(8,128)(2,1)} %param.12) | copy-start | bytes 5505028
  52.8 3.9 %copy-start.2 = (bf16[56,8,8,256]{3,2,1,0:T(8,128)(2,1)S(1)}, bf16[56,8,8,256]{3,2,1,0:T(8,128)(2,1)}, u32[]{:S(2)}) copy-start(bf16[56,8,8,256]{3,2,1,0:T(8,128)(2,1)} %copy.253) | copy-start | bytes 5505028
  52.8 3.9 %copy-start.7 = (bf16[8,8,8,256]{3,2,1,0:T(8,128)(2,1)S(1)}, bf16[8,8,8,256]{3,2,1,0:T(8,128)(2,1)}, u32[]{:S(2)}) copy-start(bf16[8,8,8,256]{3,2,1,0:T(8,128)(2,1)} %copy-done.6) | copy-start | bytes 786436
  52.8 3.9 %copy-start.10 = (f32[8,256,7]{1,2,0:T(8,128)S(1)}, f32[8,256,7]{1,2,0:T(8,128)}, u32[]{:S(2)}) copy-start(f32[8,256,7]{1,2,0:T(8,128)} %get-tuple-element.9) | copy-start | bytes 172036
  57.3 0.7 copy-start.18
  57.3 2.6 copy-start.5
  58.1 2.5 copy-start.23
  59.9 0.9 copy-start.14
  59.9 0.9 copy-start.21
  59.9 2.1 copy-start.22
  89.0 5.4 %copy-start.19 = (f32[448]{0:T(512)S(1)}, f32[448]{0:T(512)}, u32[]{:S(2)}) copy-start(f32[448]{0:T(512)} %param.18) | copy-start | bytes 5380
  120.3 0.7 copy-start.13
  120.3 0.8 copy-start.9
  120.3 2.3 copy-start.3
  129.3 6.1 %copy-start.20 = (s32[8]{0:T(128)S(1)}, s32[8]{0:T(128)}, u32[]{:S(2)}) copy-start(s32[8]{0:T(128)} %get-tuple-element.15) | copy-start | bytes 100
  139.1 75.5 %copy-start.17 = (s32[16,8]{0,1:T(8,128)S(1)}, s32[16,8]{0,1:T(8,128)}, u32[]{:S(2)}) copy-start(s32[16,8]{0,1:T(8,128)} %param.21) | copy-start | bytes 1540
  139.1 34.9 %all-to-all-start = ((bf16[16,7,4096]{2,1,0:T(8,128)(2,1)}), bf16[16,7,4096]{2,1,0:T(8,128)(2,1)}, u32[]{:S(2)}, u32[]{:S(2)}) async-start(bf16[16,7,4096]{2,1,0:T(8,128)(2,1)} %copy.224), calls=%async_computation.1 | async-start | bytes 2097152 | tf_op jit(solution)/shard_map/all_to_all | solution.py:144
  209.7 45.4 %collective-permute-start = (bf16[128,3584]{1,0:T(8,128)(2,1)}, bf16[128,3584]{1,0:T(8,128)(2,1)}, u32[]{:S(2)}, u32[]{:S(2)}) collective-permute-start(bf16[128,3584]{1,0:T(8,128)(2,1)} %constant_dynamic-slice_fusion), channel_id=1, source_target_pairs={{0,2},{2,0},{1,3},{3,1},{4,6},{6,4},{5,7},{7,5},{8,10},{10,8},{9,1... | collective-permute-start | bytes 2752520 | tf_op jit(solution)/shard_map/ppermute | solution.py:152
Sparse Core Ops, SparseCore 0:
  120.5 87.0 reduce-scatter.1
where the time goes:
time: 266 us; the launch traced here: 265 us
  waiting for transfers between devices  93.6 us (35%)
  local copies, waits for them, and re-layouts  50.7 us (19%)
  matrix products  45 us (17%)
  other arithmetic  26 us (10%)
  blocking collectives  21.6 us (8%)
  between operations  14.4 us (5%)
  starting transfers between devices  13.3 us (5%)
    ppermute x1, waiting for transfers between devices, local(): got = lax.ppermute(send, FAR_LAST, perm=[(0, 1), (1, 0)])  36.3 us
    reduce_scatter x1, waiting for transfers between devices, local(): lax.psum_scatter(partial, NEAR_FIRST, scatter_dimension=0, tiled=True)  30.8 us
    all_to_all x1, waiting for transfers between devices, local(): lax.all_to_all(outbound.astype(jnp.bfloat16), 'dp', split_axis=0, concat_...  26.5 us
    all_gather x1, blocking collectives, local(): group_stat = lax.all_gather(sum_sq, GROUP_MATES, tiled=True)  21.6 us
    dot_general x4, matrix products, split_einsum(): jnp.einsum(form, lower, narrow, preferred_element_type=jnp.float32)  14.1 us
    unnamed x62, local copies, waits for them, and re-layouts  13 us
    dot_general x1, matrix products, local(): jnp.dot(reordered, out_weight, preferred_element_type=jnp.float32)  12.6 us
    dot_general x4, matrix products, split_einsum(): first = jnp.einsum(form, upper, narrow, preferred_element_type=jnp.float32)  9.09 us
  transfers between devices with their start and end apart: 3, of which 3 were waited for; matrix products, arithmetic and copies ran while one was open for 9% of the time, Pallas kernels for 0%

commit v1 on v0

--- a/solution.py
+++ b/solution.py
@@ -117,7 +117,9 @@
     )
     gated = mixer_y * jax.nn.silu(gate_z[0].astype(jnp.float32))
     sum_sq = jnp.sum(gated * gated, axis=1)
-    group_stat = lax.all_gather(sum_sq, GROUP_MATES, tiled=True)
+    group_stat = jnp.concatenate(
+        lax.all_to_all(jnp.stack([sum_sq] * lax.axis_size(GROUP_MATES)), GROUP_MATES, 0, 0), axis=0
+    )
     mean_sq = jnp.sum(group_stat.reshape(-1, stream_len), axis=0) / (INNER // NGROUPS)
     rounded = (gated * lax.rsqrt(mean_sq + 1e-05)[:, None] * norm_gain[None, :]).astype(
         jnp.bfloat16

time: 266 us -> 244 us (0.917)
  blocking collectives: 21.6 us -> 0 us
  starting transfers between devices: 13.3 us -> 20.3 us
  local copies, waits for them, and re-layouts: 50.7 us -> 47.1 us
    all_gather x1 -> x0, blocking collectives: 21.6 us -> none  [local(): group_stat = lax.all_gather(sum_sq, GROUP_MATES, tiled=True)]
    all_to_all x0 -> x1, starting transfers between devices: none -> 8.57 us  [local(): lax.all_to_all(jnp.stack([sum_sq] * lax.axis_size(GROUP_MATES)), GROUP_MA...]
    unnamed x62 -> x48, local copies, waits for them, and re-layouts: 13 us -> 9.3 us
  transfers between devices with their start and end apart: 3 -> 4, of which waited for: 3 -> 3; matrix products, arithmetic and copies ran while one was open for 9% -> 15% of each run, Pallas kernels for 0% -> 0%
where the time goes in v1:
time: 244 us; the launch traced here: 243 us
  waiting for transfers between devices  94.7 us (39%)
  local copies, waits for them, and re-layouts  47.1 us (19%)
  matrix products  42.9 us (18%)
  other arithmetic  23.7 us (10%)
  starting transfers between devices  20.3 us (8%)
  between operations  14.4 us (6%)
    ppermute x1, waiting for transfers between devices, local(): got = lax.ppermute(send, FAR_LAST, perm=[(0, 1), (1, 0)])  36.3 us
    reduce_scatter x1, waiting for transfers between devices, local(): lax.psum_scatter(partial, NEAR_FIRST, scatter_dimension=0, tiled=True)  32.1 us
    all_to_all x1, waiting for transfers between devices, local(): lax.all_to_all(outbound.astype(jnp.bfloat16), 'dp', split_axis=0, concat_...  26.3 us
    dot_general x4, matrix products, split_einsum(): jnp.einsum(form, lower, narrow, preferred_element_type=jnp.float32)  13.2 us
    dot_general x1, matrix products, local(): jnp.dot(reordered, out_weight, preferred_element_type=jnp.float32)  12.6 us
    unnamed x48, local copies, waits for them, and re-layouts  9.3 us
    all_to_all x1, starting transfers between devices, local(): lax.all_to_all(jnp.stack([sum_sq] * lax.axis_size(GROUP_MATES)), GROUP_MA...  8.57 us
    dot_general x4, matrix products, split_einsum(): first = jnp.einsum(form, upper, narrow, preferred_element_type=jnp.float32)  8 us
  transfers between devices with their start and end apart: 4, of which 3 were waited for; matrix products, arithmetic and copies ran while one was open for 15% of the time, Pallas kernels for 0%

profile of v1, /device:TPU:32, one launch (start us, length us, event | category | flops | bytes accessed | tf_op | source)
XLA Modules:
  0.0 243.1 jit_solution(11160454687678256908)
XLA Ops:
  7.2 0.5 broadcast.241
  7.7 1.4 reduce.10
  9.3 0.7 neg.23
  9.9 0.9 multiply_bitcast_fusion
  10.8 2.0 reduce-window.6
  12.8 0.2 slice_reduce_fusion
  13.0 0.2 reduce-window.9
  13.3 0.6 copy-done.5
  14.3 0.9 dynamic-slice_reduce_fusion
  15.1 0.6 and_select_fusion
  15.7 0.7 compare_convert_fusion
  16.4 0.6 fusion.51
  17.0 0.6 copy.365
  17.7 0.6 iota_compare_fusion
  18.3 3.3 %copy.290 = bf16[56,8,8,256]{3,2,1,0:T(8,128)(2,1)} copy(bf16[56,8,8,256]{3,1,2,0:T(8,128)(2,1)} %bitcast.156) | data formatting | bytes 3670016
  21.6 0.1 copy.283
  21.8 0.8 reduce.4
  22.5 0.1 copy.284
  22.7 2.6 %constant_dynamic-slice_fusion.1 = (bf16[1,2048,64]{2,1,0:T(8,128)(2,1)}, bf16[1,2048,64]{2,1,0:T(8,128)(2,1)}) fusion(bf16[1,2048,128]{2,1,0:T(8,128)(2,1)} %param.13, s32[]{:T(128)S(6)} %select_n.54, bf16[1,2048,128]{2,1,0:T(8,128)(2,1)} %param.14), kind=kLoop, calls=%fused_computation.95 | loop fusion | bytes 1048580 | tf_op jit(solution)/shard_map/dynamic_slice | solution.py:50
  25.3 1.2 copy.280
  26.6 1.0 copy.228
  27.6 1.3 compare_and_fusion
  28.9 1.5 fusion.39
  30.4 0.1 exponential_multiply_fusion
  30.5 5.6 %fusion.4 = f32[8,7,256,64]{2,3,1,0:T(8,128)S(1)} fusion(f32[8,256,256]{2,1,0:T(8,128)S(1)} %fusion.39, f32[8,7,256]{2,1,0:T(8,128)S(1)} %get-tuple-element.10, f32[8,7,256]{2,1,0:T(8,128)S(1)} %copy.228, pred[8,256,256]{2,1,0:T(8,128)(4,1)S(1)} %compare_and_fusion, bf16[8,256,7,64]{1,0,3,2:T(8,128)(2,1)S(1)} %bitcast.150), kind=kOutput, calls=%fused_computation.7 | convolution fusion | flops 488112128 | bytes 8241152 | tf_op jit(solution)/shard_map/bhts,bshp->bthp/dot_general | solution.py:28
  36.0 6.0 %fusion.1 = f32[8,7,256,64]{2,3,1,0:T(8,128)S(1)} fusion(f32[8,256,256]{2,1,0:T(8,128)S(1)} %fusion.39, f32[8,7,256]{2,1,0:T(8,128)S(1)} %get-tuple-element.10, f32[8,7,256]{2,1,0:T(8,128)S(1)} %copy.228, pred[8,256,256]{2,1,0:T(8,128)(4,1)S(1)} %compare_and_fusion, bf16[8,256,7,64]{1,0,3,2:T(8,128)(2,1)S(1)} %bitcast.151), kind=kOutput, calls=%fused_computation.5 | convolution fusion | flops 499122176 | bytes 8241152 | tf_op jit(solution)/shard_map/bhts,bshp->bthp/dot_general | solution.py:29
  42.1 0.4 convert_element_type.197
  42.5 1.7 copy.291
  44.2 0.7 fusion.18
  44.9 0.6 fusion.28
  45.6 1.8 multiply_reduce_fusion
  47.4 0.6 fusion.37
  48.1 4.5 %multiply_reduce_fusion.1 = (f32[8,256]{1,0:T(8,128)S(1)}, f32[8,256,7,64]{1,3,2,0:T(8,128)}) fusion(f32[8,256,7,64]{1,0,3,2:T(8,128)S(1)} %bitcast.161, bf16[8,256,7,64]{1,0,3,2:T(8,128)(2,1)S(1)} %bitcast.154, f32[7]{0:T(128)S(1)} %copy-done.16, f32[8,256,7]{1,2,0:T(8,128)S(1)} %get-tuple-element.8, f32[8,256,7,64]{1,3,2,0:T(8,128)S(1)} %fusion.37, ...), kind=kOutput, calls=%fused_computation.24 | convolution fusion | flops 131201024 | bytes 21430300 | tf_op jit(solution)/shard_map/bhpn,btn->bthp/dot_general | solution.py:29
  52.5 0.7 stack.5
  53.2 8.6 %all-to-all-start = ((f32[8,1,2048]{2,1,0:T(1,128)}), f32[8,1,2048]{2,1,0:T(1,128)S(1)}, u32[]{:S(2)}, u32[]{:S(2)}) async-start(f32[8,1,2048]{2,1,0:T(1,128)} %stack.5), calls=%async_computation | async-start | bytes 131072 | tf_op jit(solution)/shard_map/all_to_all | solution.py:121
  61.8 0.2 reduce-scatter.2.cloned.1.call-start
  62.0 5.8 %reshape.362 = f32[2,2,2,2,128,448]{4,3,2,1,0,5:T(2,128)} reshape(bf16[1,2048,448]{1,2,0:T(8,128)(2,1)} %param.12) | data formatting | bytes 5505024 | tf_op jit(solution)/shard_map/convert_element_type | solution.py:118
  67.8 5.4 %reshape.357 = f32[2,2,2,2,128,448]{4,3,5,2,1,0:T(2,128)} reshape(f32[8,256,7,64]{1,3,2,0:T(8,128)} %get-tuple-element.14) | data formatting | bytes 7340032 | tf_op jit(solution)/shard_map/reshape | solution.py:95
  73.3 4.9 %fusion.27 = bf16[2,2,2,2,128,448]{4,5,2,3,1,0:T(8,128)(2,1)S(1)} fusion(f32[448]{0:T(512)S(1)} %copy-done.14, f32[2,2,2,2,128]{4,3,2,1,0:T(2,128)S(1)} %bitcast.186, f32[2,2,2,2,128,448]{4,3,2,1,0,5:T(2,128)} %reshape.362, f32[2,2,2,2,128,448]{4,3,5,2,1,0:T(2,128)} %reshape.357), kind=kLoop, calls=%fused_computation.38 | loop fusion | flops 7340032 | bytes 9185024 | tf_op jit(solution)/shard_map/transpose | solution.py:131
  78.2 3.1 %copy.258 = bf16[2,2,2,2,128,448]{4,3,2,1,0,5:T(2,128)(2,1)} copy(bf16[2,2,2,2,128,448]{4,5,2,3,1,0:T(8,128)(2,1)S(1)} %fusion.27) | data formatting | bytes 3670016 | tf_op jit(solution)/shard_map/transpose | solution.py:131
  81.3 5.3 %reshape.358 = bf16[2048,448]{0,1:T(8,128)(2,1)} reshape(bf16[2,2,2,2,128,448]{4,3,2,1,0,5:T(2,128)(2,1)} %copy.258) | data formatting | bytes 3670016 | tf_op jit(solution)/shard_map/reshape | solution.py:132
  86.6 12.6 %convolution_convert_fusion = bf16[2048,3584]{1,0:T(8,128)(2,1)} fusion(bf16[2048,448]{0,1:T(8,128)(2,1)} %reshape.358, bf16[448,3584]{1,0:T(8,128)(2,1)S(1)} %copy-done), kind=kOutput, calls=%fused_computation | convolution fusion | flops 6584008704 | bytes 19726336 | tf_op jit(solution)/shard_map/dot_general | solution.py:134
  99.2 0.7 copy-done.9
  99.8 0.1 convert_reduce_fusion
  100.0 0.2 fusion.47
  100.2 1.1 fusion.17
  101.3 0.2 broadcast_multiply_fusion
  101.5 0.7 fusion.12
  102.2 1.1 fusion.58
  103.4 2.1 convolution_add_fusion
  105.5 2.6 %reshape.359 = f32[7,64,8,64]{3,2,1,0:T(8,128)} reshape(f32[448,512]{1,0:T(8,128)} %convolution_add_fusion) | data formatting | bytes 1835008 | tf_op jit(solution)/shard_map/reshape | solution.py:114
  108.1 3.1 %copy.361 = f32[7,64,8,64]{3,1,0,2:T(8,128)} copy(f32[7,64,8,64]{3,2,1,0:T(8,128)} %reshape.359) | data formatting | bytes 1835008 | tf_op jit(solution)/shard_map/reshape | solution.py:114
  111.2 3.3 %reshape.360 = f32[8,28672]{1,0:T(8,128)} reshape(f32[8,7,64,64]{3,2,1,0:T(8,128)} %bitcast.155) | data formatting | bytes 1835008 | tf_op jit(solution)/shard_map/reshape | solution.py:116
  114.5 2.2 convolution_convert_fusion.1
  116.7 1.5 copy.260
  118.2 6.6 %all-to-all-start.1 = ((bf16[16,7,4096]{2,1,0:T(8,128)(2,1)}), bf16[16,7,4096]{2,1,0:T(8,128)(2,1)}, u32[]{:S(2)}, u32[]{:S(2)}) async-start(bf16[16,7,4096]{2,1,0:T(8,128)(2,1)} %copy.260), calls=%async_computation.2 | async-start | bytes 2097152 | tf_op jit(solution)/shard_map/all_to_all | solution.py:146
  124.8 26.3 %all-to-all-done.1 = bf16[16,7,4096]{2,1,0:T(8,128)(2,1)} async-done(((bf16[16,7,4096]{2,1,0:T(8,128)(2,1)}), bf16[16,7,4096]{2,1,0:T(8,128)(2,1)}, u32[]{:S(2)}, u32[]{:S(2)}) %all-to-all-start.1) | async-done | bytes 917536 | tf_op jit(solution)/shard_map/all_to_all | solution.py:146
  151.1 2.8 %convert_element_type.193 = f32[16,7,4096]{2,1,0:T(8,128)} convert(bf16[16,7,4096]{2,1,0:T(8,128)(2,1)} %all-to-all-done.1) | non-fusion elementwise | flops 458752 | bytes 2752512 | tf_op jit(solution)/shard_map/convert_element_type | solution.py:148
  153.9 32.1 %reduce-scatter.2.cloned.1.call-done = bf16[256,3584]{1,0:T(8,128)(2,1)} async-done(((bf16[2048,3584]{1,0:T(8,128)(2,1)}), bf16[256,3584]{1,0:T(8,128)(2,1)}) %reduce-scatter.2.cloned.1.call-update) | async-done | bytes 1835024 | tf_op jit(solution)/shard_map/reduce_scatter | solution.py:137
  186.0 2.2 constant_dynamic-slice_fusion
  188.2 4.8 %collective-permute-start = (bf16[128,3584]{1,0:T(8,128)(2,1)}, bf16[128,3584]{1,0:T(8,128)(2,1)}, u32[]{:S(2)}, u32[]{:S(2)}) collective-permute-start(bf16[128,3584]{1,0:T(8,128)(2,1)} %constant_dynamic-slice_fusion), channel_id=1, source_target_pairs={{0,2},{2,0},{1,3},{3,1},{4,6},{6,4},{5,7},{7,5},{8,10},{10,8},{9,1... | collective-permute-start | bytes 2752520 | tf_op jit(solution)/shard_map/ppermute | solution.py:154
  193.1 4.2 %fusion.20 = f32[8,7,4096]{2,0,1:T(8,128)} fusion(pred[16,8]{0,1:T(8,128)(4,1)S(1)} %compare_reduce_fusion, f32[2,8,7,4096]{3,2,1,0:T(8,128)} %bitcast.149), kind=kOutput, calls=%fused_computation.30 | convolution fusion | flops 44040192 | bytes 2752640 | tf_op jit(solution)/shard_map/dot_general | solution.py:159
  197.3 36.3 %collective-permute-done = bf16[128,3584]{1,0:T(8,128)(2,1)} collective-permute-done((bf16[128,3584]{1,0:T(8,128)(2,1)}, bf16[128,3584]{1,0:T(8,128)(2,1)}, u32[]{:S(2)}, u32[]{:S(2)}) %collective-permute-start) | collective-permute-done | bytes 917536 | tf_op jit(solution)/shard_map/ppermute | solution.py:154
  233.6 2.6 %fusion.35 = bf16[1,128,3584]{2,1,0:T(8,128)(2,1)} fusion(bf16[128,3584]{1,0:T(8,128)(2,1)} %collective-permute-done, bf16[256,3584]{1,0:T(8,128)(2,1)} %reduce-scatter.2.cloned.1.call-done, s32[]{:T(128)S(6)} %select_n.58), kind=kLoop, calls=%fused_computation.46 | loop fusion | flops 1835008 | bytes 2752516 | tf_op jit(solution)/shard_map/broadcast_in_dim | solution.py:156
  (55 shorter events, 1.0 us)
Async XLA Ops:
  7.2 79.4 %copy-start = (bf16[448,3584]{1,0:T(8,128)(2,1)S(1)}, bf16[448,3584]{1,0:T(8,128)(2,1)}, u32[]{:S(2)}) copy-start(bf16[448,3584]{1,0:T(8,128)(2,1)} %param.19) | copy-start | bytes 9633796
  7.2 14.6 %copy-start.8 = (f32[1,2048,7]{1,0,2:T(1,128)S(1)}, f32[1,2048,7]{1,0,2:T(1,128)}, u32[]{:S(2)}) copy-start(f32[1,2048,7]{1,0,2:T(1,128)} %param.15) | copy-start | bytes 172036
  13.3 0.6 copy-start.5
  26.5 3.8 %copy-start.7 = (f32[2048,7]{0,1:T(8,128)S(1)}, f32[2048,7]{0,1:T(8,128)}, u32[]{:S(2)}) copy-start(f32[2048,7]{0,1:T(8,128)} %reduce.4) | copy-start | bytes 172036
  26.5 3.8 %copy-start.10 = (f32[8,256]{1,0:T(8,128)S(1)}, f32[8,256]{1,0:T(8,128)}, u32[]{:S(2)}) copy-start(f32[8,256]{1,0:T(8,128)} %get-tuple-element.11) | copy-start | bytes 24580
  26.5 3.8 %copy-start.11 = (f32[8,256]{1,0:T(8,128)S(1)}, f32[8,256]{1,0:T(8,128)}, u32[]{:S(2)}) copy-start(f32[8,256]{1,0:T(8,128)} %get-tuple-element.12) | copy-start | bytes 24580
  26.5 3.9 %copy-start.1 = (bf16[56,8,8,256]{3,2,1,0:T(8,128)(2,1)S(1)}, bf16[56,8,8,256]{3,2,1,0:T(8,128)(2,1)}, u32[]{:S(2)}) copy-start(bf16[56,8,8,256]{3,2,1,0:T(8,128)(2,1)} %copy.290) | copy-start | bytes 5505028
  36.0 6.0 %copy-start.3 = (bf16[1,2048,448]{1,2,0:T(8,128)(2,1)S(1)}, bf16[1,2048,448]{1,2,0:T(8,128)(2,1)}, u32[]{:S(2)}) copy-start(bf16[1,2048,448]{1,2,0:T(8,128)(2,1)} %param.12) | copy-start | bytes 5505028
  44.9 0.7 copy-start.13
  44.9 2.5 %copy-start.4 = (bf16[1,2048,64]{2,1,0:T(8,128)(2,1)S(1)}, bf16[1,2048,64]{2,1,0:T(8,128)(2,1)}, u32[]{:S(2)}) copy-start(bf16[1,2048,64]{2,1,0:T(8,128)(2,1)} %get-tuple-element.18) | copy-start | bytes 786436
  47.4 0.7 copy-start.16
  53.2 20.0 %all-to-all-start = ((f32[8,1,2048]{2,1,0:T(1,128)}), f32[8,1,2048]{2,1,0:T(1,128)S(1)}, u32[]{:S(2)}, u32[]{:S(2)}) async-start(f32[8,1,2048]{2,1,0:T(1,128)} %stack.5), calls=%async_computation | async-start | bytes 131072 | tf_op jit(solution)/shard_map/all_to_all | solution.py:121
  61.8 124.3 %reduce-scatter.2.cloned.1.call-start = ((), (), s32[]{:S(2)}) async-start(), calls=%async_computation.3 | async-start | bytes 16515072 | tf_op jit(solution)/shard_map/reduce_scatter | solution.py:137
  67.8 5.5 %copy-start.14 = (f32[448]{0:T(512)S(1)}, f32[448]{0:T(512)}, u32[]{:S(2)}) copy-start(f32[448]{0:T(512)} %param.18) | copy-start | bytes 5380
  99.1 0.7 copy-start.9
  99.1 0.8 copy-start.6
  99.2 2.3 copy-start.2
  108.1 6.4 %copy-start.15 = (s32[8]{0:T(128)S(1)}, s32[8]{0:T(128)}, u32[]{:S(2)}) copy-start(s32[8]{0:T(128)} %get-tuple-element.15) | copy-start | bytes 100
  118.2 74.9 %copy-start.12 = (s32[16,8]{0,1:T(8,128)S(1)}, s32[16,8]{0,1:T(8,128)}, u32[]{:S(2)}) copy-start(s32[16,8]{0,1:T(8,128)} %param.21) | copy-start | bytes 1540
  118.2 32.9 %all-to-all-start.1 = ((bf16[16,7,4096]{2,1,0:T(8,128)(2,1)}), bf16[16,7,4096]{2,1,0:T(8,128)(2,1)}, u32[]{:S(2)}, u32[]{:S(2)}) async-start(bf16[16,7,4096]{2,1,0:T(8,128)(2,1)} %copy.260), calls=%async_computation.2 | async-start | bytes 2097152 | tf_op jit(solution)/shard_map/all_to_all | solution.py:146
  188.2 45.4 %collective-permute-start = (bf16[128,3584]{1,0:T(8,128)(2,1)}, bf16[128,3584]{1,0:T(8,128)(2,1)}, u32[]{:S(2)}, u32[]{:S(2)}) collective-permute-start(bf16[128,3584]{1,0:T(8,128)(2,1)} %constant_dynamic-slice_fusion), channel_id=1, source_target_pairs={{0,2},{2,0},{1,3},{3,1},{4,6},{6,4},{5,7},{7,5},{8,10},{10,8},{9,1... | collective-permute-start | bytes 2752520 | tf_op jit(solution)/shard_map/ppermute | solution.py:154
Sparse Core Ops, SparseCore 0:
  99.3 86.7 reduce-scatter.1
